TPU v7x, 256 devices: a whole 4x4x8 slice. The times are simulated.
256 devices in a mesh: gx: 16 (over z, core), gy: 16 (over x, y).
Axes of the slice: x: 4, y: 4, z: 8, core: 2. Of those that a mesh axis runs over, the one named last changes fastest.
Arguments:
- state: bfloat16 [2, 256, 768, 2048], P(None, None, 'gx', 'gy'), as said below
Outputs:
- modes: bfloat16 [255, 2, 768, 2048], P(None, None, 'gx', 'gy')
- reduced: float32 [255, 255], replicated
Inputs may be any that keep to these rules, and one draw needn't show every extreme that they name: `state`: both fields are positive.
All inputs are finite; a program needn't handle non-finite values.
Results may differ from a plain program's by a relative error of at most 0.0077.
Values may be sent and summed in bfloat16 or wider, within the bound.
No kernel may reach another device: no remote copies, remote signals or barrier semaphores. Data moves between devices by JAX's collectives and lax.ppermute only.
A program may use at most 128 MiB of HBM per device.

v0:
```python
import jax
import jax.numpy as jnp
from jax import lax
from jax.sharding import PartitionSpec as P


def padded_2(cells, sides, width):
    for axis, dim in sides:
        count = lax.axis_size(axis)
        ends = count - 1
        head = lax.slice_in_dim(cells, 0, width, axis=dim)
        tail = lax.slice_in_dim(cells, cells.shape[dim] - width, cells.shape[dim], axis=dim)
        cells = jnp.concatenate(
            [
                lax.ppermute(tail, axis, [(i, (i + 1) % count) for i in range(ends)]),
                cells,
                lax.ppermute(head, axis, [((i + 1) % count, i) for i in range(ends)]),
            ],
            axis=dim,
        )
    return cells


def tri_solve(lower, right):
    return lax.linalg.triangular_solve(lower, right, left_side=True, lower=True)


def gradients(padded):
    grad_x = (
        padded[:, :-4, 2:-2]
        - 8.0 * padded[:, 1:-3, 2:-2]
        + 8.0 * padded[:, 3:-1, 2:-2]
        - padded[:, 4:, 2:-2]
    ) / 12.0
    grad_y = (
        padded[:, 2:-2, :-4]
        - 8.0 * padded[:, 2:-2, 1:-3]
        + 8.0 * padded[:, 2:-2, 3:-1]
        - padded[:, 2:-2, 4:]
    ) / 12.0
    return jnp.stack([grad_x, grad_y], axis=1).astype(jnp.bfloat16)


def shards(state):
    snaps = state.shape[1]
    rows_x = state.shape[2]
    rows_y = state.shape[3]
    total_rows = 2 * rows_x * rows_y * lax.axis_size("gx") * lax.axis_size("gy")
    temp = 0.4 * state[1].astype(jnp.float32) / state[0].astype(jnp.float32)
    padded = padded_2(temp, (("gx", 1), ("gy", 2)), 2)
    features = gradients(padded)
    snap = features.reshape(snaps, 2 * rows_x * rows_y)
    local_gram = (
        lax.dot_general(snap, snap, (((1,), (1,)), ((), ())), preferred_element_type=jnp.float32)
        / total_rows
    )
    gram = lax.psum(local_gram, ("gx", "gy"))
    lower = jnp.linalg.cholesky(gram[: snaps - 1, : snaps - 1])
    cross = gram[: snaps - 1, 1:]
    half = tri_solve(lower, cross)
    reduced = tri_solve(lower, half.T).T
    inverse = tri_solve(lower, jnp.eye(snaps - 1, dtype=jnp.float32)).astype(jnp.bfloat16)
    modes = jnp.dot(inverse, snap[1:], preferred_element_type=jnp.float32).astype(jnp.bfloat16)
    return (modes.reshape(snaps - 1, 2, rows_x, rows_y), reduced)


def solution(mesh):
    placed = (P(None, None, "gx", "gy"),)
    return jax.shard_map(
        shards,
        mesh=mesh,
        in_specs=placed,
        out_specs=(P(None, None, "gx", "gy"), P()),
        check_vma=False,
    )
```

profile of v0, /device:TPU:2, one launch (start us, length us, event | category | flops | bytes accessed | tf_op | source)
XLA Modules:
  0.0 435.9 jit_solution(15575594914575890213)
XLA Ops:
  7.2 3.9 fusion.44
  11.1 1.3 divide_bitcast_fusion
  12.5 1.8 collective-permute-start
  14.3 1.3 collective-permute-start.1
  16.3 3.1 collective-permute-done.1
  20.1 3.6 pad_maximum_fusion.1
  23.7 11.6 %fusion.42 = (f32[256,52,2]{2,0,1:T(8,128)}, f32[256,52,2]{2,0,1:T(8,128)}) fusion(f32[256,52,128]{2,0,1:T(8,128)} %pad_maximum_fusion.1), kind=kLoop, calls=%fused_computation.88 | loop fusion | bytes 425984 | tf_op jit(solution)/shard_map/slice | solution.py:12
  35.4 4.7 %copy.16 = f32[256,52,2]{0,2,1:T(2,128)S(1)} copy(f32[256,52,2]{2,0,1:T(8,128)} %get-tuple-element.41) | data formatting | bytes 212992 | tf_op jit(solution)/shard_map/slice | solution.py:12
  40.1 3.5 collective-permute-start.2
  43.6 5.3 %copy.18 = f32[256,52,2]{0,2,1:T(2,128)} copy(f32[256,52,2]{2,0,1:T(8,128)} %get-tuple-element.42) | data formatting | bytes 212992 | tf_op jit(solution)/shard_map/slice | solution.py:11
  48.9 4.6 %collective-permute-start.3 = (f32[256,52,2]{0,2,1:T(2,128)}, f32[256,52,2]{0,2,1:T(2,128)}, u32[]{:S(2)}, u32[]{:S(2)}) collective-permute-start(f32[256,52,2]{0,2,1:T(2,128)} %copy.18), channel_id=1, source_target_pairs={{1,0},{2,1},{3,2},{4,3},{5,4},{6,5},{7,6},{8,7},{9,8},{10,9},{11,1... | collective-permute-start | bytes 319496 | tf_op jit(solution)/shard_map/ppermute | solution.py:17
  53.5 11.1 %fusion.17 = bf16[256,1,48,128]{3,0,2,1:T(8,128)(2,1)S(1)} fusion(f32[256,2,128]{2,0,1:T(8,128)} %copy-done.2, f32[256,48,128]{2,0,1:T(8,128)} %copy-done, f32[256,2,128]{2,0,1:T(8,128)S(1)} %collective-permute-done), kind=kLoop, calls=%fused_computation.36 | loop fusion | flops 17301504 | bytes 9961472 | tf_op jit(solution)/shard_map/stack | solution.py:41
  64.6 5.0 %copy.17 = f32[256,52,2]{2,0,1:T(8,128)} copy(f32[256,52,2]{0,2,1:T(2,128)} %collective-permute-done.2) | data formatting | bytes 212992 | tf_op jit(solution)/shard_map/ppermute | solution.py:15
  69.6 5.1 %copy.19 = f32[256,52,2]{2,0,1:T(8,128)} copy(f32[256,52,2]{0,2,1:T(2,128)} %collective-permute-done.3) | data formatting | bytes 212992 | tf_op jit(solution)/shard_map/ppermute | solution.py:17
  74.7 21.0 %fusion.18 = bf16[256,1,48,128]{3,0,2,1:T(8,128)(2,1)S(1)} fusion(f32[256,52,2]{2,0,1:T(8,128)} %copy.19, f32[256,2,128]{2,0,1:T(8,128)} %copy-done.2, f32[256,48,128]{2,0,1:T(8,128)} %copy-done, f32[256,2,128]{2,0,1:T(8,128)S(1)} %collective-permute-done, f32[256,52,2]{2,0,1:T(8,128)} %copy.17), kind=kLoop, calls=%fused_computation.37 | loop fusion | flops 29884416 | bytes 10174464 | tf_op jit(solution)/shard_map/stack | solution.py:41
  95.8 1.7 copy-done.1
  97.4 2.5 fusion.20
  100.0 5.9 %fusion.8 = bf16[255,2,48,128]{3,0,2,1:T(8,128)(2,1)} fusion(bf16[256,1,48,128]{3,0,2,1:T(8,128)(2,1)S(1)} %fusion.17, bf16[256,1,48,128]{3,0,2,1:T(8,128)(2,1)} %copy-done.1), kind=kLoop, calls=%fused_computation.17 | loop fusion | flops 3133440 | bytes 12558336 | tf_op jit(solution)/shard_map/stack | solution.py:41
  105.8 8.7 %copy.22 = bf16[255,2,48,128]{0,3,2,1:T(8,128)(2,1)} copy(bf16[255,2,48,128]{3,0,2,1:T(8,128)(2,1)} %fusion.8) | data formatting | bytes 12533760 | tf_op jit(solution)/shard_map/slice | solution.py:63
  114.5 240.5 %all-reduce.4.cloned.1.call-done = f32[256,256]{0,1:T(8,128)} async-done(((f32[256,256]{0,1:T(8,128)}), f32[256,256]{0,1:T(8,128)}) %all-reduce.4.cloned.1.call-update) | async-done | bytes 262160 | tf_op jit(solution)/shard_map/psum | solution.py:57
  355.0 1.1 copy.21
  356.1 1.0 fusion.21
  357.1 11.7 %cholesky.51 = f32[128,128]{1,0:T(8,128)S(1)} custom-call(f32[128,128]{1,0:T(8,128)S(1)} %cholesky.124), custom_call_target="Cholesky" | custom-call | tf_op jit(solution)/shard_map/jit(cholesky)/cholesky | solution.py:58
  368.9 9.8 %custom-call.14 = f32[1,128,128]{1,2,0:T(8,128)S(1)} custom-call(f32[1,128,128]{2,1,0:T(8,128)S(1)} %get-tuple-element.50), custom_call_target="InvertDiagBlocksLowerTriangular" | custom-call | tf_op jit(solution)/shard_map/jit(cholesky)/cholesky | solution.py:58
  379.2 11.6 %cholesky.110 = f32[127,127]{1,0:T(8,128)S(1)} custom-call(f32[127,127]{1,0:T(8,128)S(1)} %convolution_subtract_fusion.2), custom_call_target="Cholesky" | custom-call | tf_op jit(solution)/shard_map/jit(cholesky)/cholesky | solution.py:58
  393.6 19.9 %custom-call.17 = f32[2,128,128]{1,2,0:T(8,128)S(1)} custom-call(f32[2,128,128]{2,1,0:T(8,128)S(1)} %pad_maximum_fusion.15), custom_call_target="InvertDiagBlocksLowerTriangular" | custom-call | tf_op jit(solution)/shard_map/triangular_solve/custom-call.0 | solution.py:25
  413.5 1.2 fusion.26
  415.1 1.2 fusion.25
  417.4 0.8 copy.25
  419.2 4.6 %convolution_convert_fusion = bf16[255,12288]{1,0:T(8,128)(2,1)S(1)} fusion(bf16[255,12288]{0,1:T(8,128)(2,1)} %bitcast.61, bf16[127,255]{1,0:T(8,128)(2,1)S(1)} %fusion.35, f32[128,255]{1,0:T(8,128)S(1)} %fusion.28), kind=kOutput, calls=%fused_computation | convolution fusion | flops 1601447936 | bytes 12729090 | tf_op jit(solution)/shard_map/dot_general | solution.py:63
  423.8 1.5 copy.32
  425.3 3.8 slice.212
  (37 shorter events, 5.8 us)
Async XLA Ops:
  7.2 347.8 %all-reduce.4.cloned.1.call-start = ((), (), s32[]{:S(2)}) async-start(), calls=%async_computation | async-start | bytes 524288 | tf_op jit(solution)/shard_map/psum | solution.py:57
  12.5 6.9 %copy-start = (f32[256,48,128]{2,0,1:T(8,128)}, f32[256,48,128]{2,0,1:T(8,128)S(1)}, u32[]{:S(2)}) copy-start(f32[256,48,128]{2,0,1:T(8,128)S(1)} %divide_bitcast_fusion) | copy-start | bytes 18874372
  12.5 3.8 collective-permute-start
  14.3 5.1 %collective-permute-start.1 = (f32[256,2,128]{2,0,1:T(8,128)S(1)}, f32[256,2,128]{2,0,1:T(8,128)S(1)}, u32[]{:S(2)}, u32[]{:S(2)}) collective-permute-start(f32[256,2,128]{2,0,1:T(8,128)S(1)} %get-tuple-element.44), channel_id=1, source_target_pairs={{16,0},{32,16},{48,32},{64,48},{80,64},{96,80},{112,96},{128,112},... | collective-permute-start | bytes 786440 | tf_op jit(solution)/shard_map/ppermute | solution.py:17
  19.4 0.7 copy-start.2
  40.1 24.5 %collective-permute-start.2 = (f32[256,52,2]{0,2,1:T(2,128)S(1)}, f32[256,52,2]{0,2,1:T(2,128)}, u32[]{:S(2)}, u32[]{:S(2)}) collective-permute-start(f32[256,52,2]{0,2,1:T(2,128)S(1)} %copy.16), channel_id=1, source_target_pairs={{0,1},{1,2},{2,3},{3,4},{4,5},{5,6},{6,7},{7,8},{8,9},{9,10},{10,1... | collective-permute-start | bytes 319496 | tf_op jit(solution)/shard_map/ppermute | solution.py:15
  48.9 20.7 %collective-permute-start.3 = (f32[256,52,2]{0,2,1:T(2,128)}, f32[256,52,2]{0,2,1:T(2,128)}, u32[]{:S(2)}, u32[]{:S(2)}) collective-permute-start(f32[256,52,2]{0,2,1:T(2,128)} %copy.18), channel_id=1, source_target_pairs={{1,0},{2,1},{3,2},{4,3},{5,4},{6,5},{7,6},{8,7},{9,8},{10,9},{11,1... | collective-permute-start | bytes 319496 | tf_op jit(solution)/shard_map/ppermute | solution.py:17
  95.8 1.7 copy-start.1
  105.8 287.6 %copy-start.4 = (f32[128,1]{1,0:T(8,128)S(1)}, f32[128,1]{1,0:T(8,128)}, u32[]{:S(2)}) copy-start(f32[128,1]{1,0:T(8,128)} %constant.87.clone.3) | copy-start | bytes 1540
  114.5 303.8 %copy-start.3 = (f32[255,255]{1,0:T(8,128)S(1)}, f32[255,255]{1,0:T(8,128)}, u32[]{:S(2)}) copy-start(f32[255,255]{1,0:T(8,128)} %fusion.22) | copy-start | bytes 780304
Sparse Core Ops, SparseCore 0:
  100.1 254.8 all-reduce.3
where the time goes:
time: 437 us; the launch traced here: 436 us
  waiting for transfers between devices  244 us (56%)
  other arithmetic  99.2 us (23%)
  local copies, waits for them, and re-layouts  53.9 us (12%)
  between operations  15.6 us (4%)
  matrix products  12.3 us (3%)
  starting transfers between devices  11.2 us (3%)
    psum x1, waiting for transfers between devices, shards(): gram = lax.psum(local_gram, ('gx', 'gy'))  240 us
    another operation x3, other arithmetic, gradients(): return jnp.stack([grad_x, grad_y], axis=1).astype(jnp.bfloat16)  38 us
    another operation x7, other arithmetic, shards(): lower = jnp.linalg.cholesky(gram[:snaps - 1, :snaps - 1])  34.5 us
    another operation x4, other arithmetic, tri_solve(): return lax.linalg.triangular_solve(lower, right, left_side=True, lower=True)  20.1 us
    slice x3, local copies, waits for them, and re-layouts, padded_2(): lax.slice_in_dim(cells, cells.shape[dim] - width, cells.shape[dim], axis=...  16.4 us
  transfers between devices with their start and end apart: 5, of which 2 were waited for; matrix products, arithmetic and copies ran while one was open for 8% of the time, Pallas kernels for 0%

commit v1 on v0

--- a/solution.py
+++ b/solution.py
@@ -54,7 +54,7 @@
         lax.dot_general(snap, snap, (((1,), (1,)), ((), ())), preferred_element_type=jnp.float32)
         / total_rows
     )
-    gram = lax.psum(local_gram, ("gx", "gy"))
+    gram = jnp.sum(lax.all_gather(local_gram, ("gx", "gy")), axis=0)
     lower = jnp.linalg.cholesky(gram[: snaps - 1, : snaps - 1])
     cross = gram[: snaps - 1, 1:]
     half = tri_solve(lower, cross)

time: 437 us -> 418 us (0.957)
  waiting for transfers between devices: 244 us -> 207 us
  other arithmetic: 99.2 us -> 119 us
    psum x1 -> x0, waiting for transfers between devices: 240 us -> none  [shards(): gram = lax.psum(local_gram, ('gx', 'gy'))]
    all_gather x0 -> x1, waiting for transfers between devices: none -> 203 us  [shards(): gram = jnp.sum(lax.all_gather(local_gram, ('gx', 'gy')), axis=0)]
    reduce_sum x0 -> x1, other arithmetic: none -> 21.3 us  [shards(): gram = jnp.sum(lax.all_gather(local_gram, ('gx', 'gy')), axis=0)]
  transfers between devices with their start and end apart: 5 -> 5, of which waited for: 2 -> 2; matrix products, arithmetic and copies ran while one was open for 8% -> 9% of each run, Pallas kernels for 0% -> 0%
where the time goes in v1:
time: 418 us; the launch traced here: 416 us
  waiting for transfers between devices  207 us (50%)
  other arithmetic  119 us (28%)
  local copies, waits for them, and re-layouts  52.9 us (13%)
  between operations  15.6 us (4%)
  starting transfers between devices  11.2 us (3%)
  matrix products  10.4 us (2%)
    all_gather x1, waiting for transfers between devices, shards(): gram = jnp.sum(lax.all_gather(local_gram, ('gx', 'gy')), axis=0)  203 us
    another operation x3, other arithmetic, gradients(): return jnp.stack([grad_x, grad_y], axis=1).astype(jnp.bfloat16)  38.2 us
    another operation x7, other arithmetic, shards(): lower = jnp.linalg.cholesky(gram[:snaps - 1, :snaps - 1])  34.5 us
    reduce_sum x1, other arithmetic, shards(): gram = jnp.sum(lax.all_gather(local_gram, ('gx', 'gy')), axis=0)  21.3 us
    another operation x4, other arithmetic, tri_solve(): return lax.linalg.triangular_solve(lower, right, left_side=True, lower=True)  20.1 us
    slice x3, local copies, waits for them, and re-layouts, padded_2(): lax.slice_in_dim(cells, cells.shape[dim] - width, cells.shape[dim], axis=...  16.4 us
    slice x1, local copies, waits for them, and re-layouts, shards(): snap[1:]  8.65 us
    unnamed x12, local copies, waits for them, and re-layouts  8.57 us
  transfers between devices with their start and end apart: 5, of which 2 were waited for; matrix products, arithmetic and copies ran while one was open for 9% of the time, Pallas kernels for 0%

profile of v1, /device:TPU:2, one launch (start us, length us, event | category | flops | bytes accessed | tf_op | source)
XLA Modules:
  0.0 415.8 jit_solution(17109932778498276445)
XLA Ops:
  7.2 3.9 fusion.43
  11.1 1.3 divide_bitcast_fusion
  12.5 1.8 collective-permute-start
  14.3 1.3 collective-permute-start.1
  15.6 3.8 collective-permute-done.1
  19.4 0.7 copy-done.2
  20.1 3.6 pad_maximum_fusion.1
  23.7 11.6 %fusion.41 = (f32[256,52,2]{2,0,1:T(8,128)}, f32[256,52,2]{2,0,1:T(8,128)}) fusion(f32[256,52,128]{2,0,1:T(8,128)} %pad_maximum_fusion.1), kind=kLoop, calls=%fused_computation.87 | loop fusion | bytes 425984 | tf_op jit(solution)/shard_map/slice | solution.py:12
  35.4 4.7 %copy.14 = f32[256,52,2]{0,2,1:T(2,128)S(1)} copy(f32[256,52,2]{2,0,1:T(8,128)} %get-tuple-element.41) | data formatting | bytes 212992 | tf_op jit(solution)/shard_map/slice | solution.py:12
  40.1 3.5 collective-permute-start.2
  43.6 5.3 %copy.16 = f32[256,52,2]{0,2,1:T(2,128)} copy(f32[256,52,2]{2,0,1:T(8,128)} %get-tuple-element.42) | data formatting | bytes 212992 | tf_op jit(solution)/shard_map/slice | solution.py:11
  48.9 4.6 %collective-permute-start.3 = (f32[256,52,2]{0,2,1:T(2,128)}, f32[256,52,2]{0,2,1:T(2,128)}, u32[]{:S(2)}, u32[]{:S(2)}) collective-permute-start(f32[256,52,2]{0,2,1:T(2,128)} %copy.16), channel_id=1, source_target_pairs={{1,0},{2,1},{3,2},{4,3},{5,4},{6,5},{7,6},{8,7},{9,8},{10,9},{11,1... | collective-permute-start | bytes 319496 | tf_op jit(solution)/shard_map/ppermute | solution.py:17
  53.5 11.1 %fusion.17 = bf16[256,1,48,128]{3,0,2,1:T(8,128)(2,1)S(1)} fusion(f32[256,2,128]{2,0,1:T(8,128)} %copy-done.2, f32[256,48,128]{2,0,1:T(8,128)} %copy-done, f32[256,2,128]{2,0,1:T(8,128)S(1)} %collective-permute-done), kind=kLoop, calls=%fused_computation.36 | loop fusion | flops 17301504 | bytes 9961472 | tf_op jit(solution)/shard_map/stack | solution.py:41
  64.6 5.0 %copy.15 = f32[256,52,2]{2,0,1:T(8,128)} copy(f32[256,52,2]{0,2,1:T(2,128)} %collective-permute-done.2) | data formatting | bytes 212992 | tf_op jit(solution)/shard_map/ppermute | solution.py:15
  69.6 5.1 %copy.17 = f32[256,52,2]{2,0,1:T(8,128)} copy(f32[256,52,2]{0,2,1:T(2,128)} %collective-permute-done.3) | data formatting | bytes 212992 | tf_op jit(solution)/shard_map/ppermute | solution.py:17
  74.7 21.3 %fusion.18 = bf16[256,1,48,128]{3,0,2,1:T(8,128)(2,1)S(1)} fusion(f32[256,52,2]{2,0,1:T(8,128)} %copy.17, f32[256,2,128]{2,0,1:T(8,128)} %copy-done.2, f32[256,48,128]{2,0,1:T(8,128)} %copy-done, f32[256,2,128]{2,0,1:T(8,128)S(1)} %collective-permute-done, f32[256,52,2]{2,0,1:T(8,128)} %copy.15), kind=kLoop, calls=%fused_computation.37 | loop fusion | flops 29884416 | bytes 10174464 | tf_op jit(solution)/shard_map/stack | solution.py:41
  96.0 1.7 copy-done.1
  97.6 2.5 fusion.20
  100.2 5.9 %fusion.8 = bf16[255,2,48,128]{3,0,2,1:T(8,128)(2,1)} fusion(bf16[256,1,48,128]{3,0,2,1:T(8,128)(2,1)S(1)} %fusion.17, bf16[256,1,48,128]{3,0,2,1:T(8,128)(2,1)} %copy-done.1), kind=kLoop, calls=%fused_computation.17 | loop fusion | flops 3133440 | bytes 12558336 | tf_op jit(solution)/shard_map/stack | solution.py:41
  106.1 8.6 %copy.20 = bf16[255,2,48,128]{0,3,2,1:T(8,128)(2,1)} copy(bf16[255,2,48,128]{3,0,2,1:T(8,128)(2,1)} %fusion.8) | data formatting | bytes 12533760 | tf_op jit(solution)/shard_map/slice | solution.py:63
  114.7 202.7 %all-gather.3.cloned.1.call-done = f32[65536,256]{1,0:T(8,128)} async-done(((f32[256,256]{1,0:T(8,128)}), f32[65536,256]{1,0:T(8,128)}) %all-gather.3.cloned.1.call-update) | async-done | bytes 67108880 | tf_op jit(solution)/shard_map/all_gather | solution.py:57
  317.4 21.3 %reduce_sum.9 = f32[256,256]{1,0:T(8,128)S(1)} reduce(f32[256,256,256]{2,1,0:T(8,128)} %bitcast.5, f32[]{:T(128)} %constant.93.clone.1), dimensions={0}, to_apply=%region_0.0 | reduce | flops 16711680 | bytes 67371008 | tf_op jit(solution)/shard_map/reduce_sum | solution.py:57
  338.9 11.7 %cholesky.51 = f32[128,128]{1,0:T(8,128)S(1)} custom-call(f32[128,128]{1,0:T(8,128)S(1)} %cholesky.124), custom_call_target="Cholesky" | custom-call | tf_op jit(solution)/shard_map/jit(cholesky)/cholesky | solution.py:58
  350.7 9.8 %custom-call.14 = f32[1,128,128]{1,2,0:T(8,128)S(1)} custom-call(f32[1,128,128]{2,1,0:T(8,128)S(1)} %get-tuple-element.50), custom_call_target="InvertDiagBlocksLowerTriangular" | custom-call | tf_op jit(solution)/shard_map/jit(cholesky)/cholesky | solution.py:58
  361.0 11.6 %cholesky.110 = f32[127,127]{1,0:T(8,128)S(1)} custom-call(f32[127,127]{1,0:T(8,128)S(1)} %convolution_subtract_fusion.3), custom_call_target="Cholesky" | custom-call | tf_op jit(solution)/shard_map/jit(cholesky)/cholesky | solution.py:58
  372.6 0.6 compare_reduce_fusion
  373.3 0.6 compare_reduce_fusion.1
  375.4 19.9 %custom-call.17 = f32[2,128,128]{1,2,0:T(8,128)S(1)} custom-call(f32[2,128,128]{2,1,0:T(8,128)S(1)} %pad_maximum_fusion.15), custom_call_target="InvertDiagBlocksLowerTriangular" | custom-call | tf_op jit(solution)/shard_map/triangular_solve/custom-call.0 | solution.py:25
  397.4 0.8 copy.22
  399.1 4.6 %convolution_convert_fusion = bf16[255,12288]{1,0:T(8,128)(2,1)S(1)} fusion(bf16[255,12288]{0,1:T(8,128)(2,1)} %bitcast.65, bf16[127,255]{1,0:T(8,128)(2,1)S(1)} %fusion.35, f32[128,255]{1,0:T(8,128)S(1)} %fusion.27), kind=kOutput, calls=%fused_computation | convolution fusion | flops 1601447936 | bytes 12729090 | tf_op jit(solution)/shard_map/dot_general | solution.py:63
  403.7 1.5 copy.28
  405.2 3.8 slice.212
  (36 shorter events, 3.9 us)
Async XLA Ops:
  7.2 310.3 %all-gather.3.cloned.1.call-start = ((), (), s32[]{:S(2)}) async-start(), calls=%async_computation | async-start | bytes 67371008 | tf_op jit(solution)/shard_map/all_gather | solution.py:57
  12.5 6.9 %copy-start = (f32[256,48,128]{2,0,1:T(8,128)}, f32[256,48,128]{2,0,1:T(8,128)S(1)}, u32[]{:S(2)}) copy-start(f32[256,48,128]{2,0,1:T(8,128)S(1)} %divide_bitcast_fusion) | copy-start | bytes 18874372
  12.5 3.1 collective-permute-start
  14.3 5.1 %collective-permute-start.1 = (f32[256,2,128]{2,0,1:T(8,128)S(1)}, f32[256,2,128]{2,0,1:T(8,128)S(1)}, u32[]{:S(2)}, u32[]{:S(2)}) collective-permute-start(f32[256,2,128]{2,0,1:T(8,128)S(1)} %get-tuple-element.44), channel_id=1, source_target_pairs={{16,0},{32,16},{48,32},{64,48},{80,64},{96,80},{112,96},{128,112},... | collective-permute-start | bytes 786440 | tf_op jit(solution)/shard_map/ppermute | solution.py:17
  19.4 0.7 copy-start.2
  40.1 24.5 %collective-permute-start.2 = (f32[256,52,2]{0,2,1:T(2,128)S(1)}, f32[256,52,2]{0,2,1:T(2,128)}, u32[]{:S(2)}, u32[]{:S(2)}) collective-permute-start(f32[256,52,2]{0,2,1:T(2,128)S(1)} %copy.14), channel_id=1, source_target_pairs={{0,1},{1,2},{2,3},{3,4},{4,5},{5,6},{6,7},{7,8},{8,9},{9,10},{10,1... | collective-permute-start | bytes 319496 | tf_op jit(solution)/shard_map/ppermute | solution.py:15
  48.9 20.7 %collective-permute-start.3 = (f32[256,52,2]{0,2,1:T(2,128)}, f32[256,52,2]{0,2,1:T(2,128)}, u32[]{:S(2)}, u32[]{:S(2)}) collective-permute-start(f32[256,52,2]{0,2,1:T(2,128)} %copy.16), channel_id=1, source_target_pairs={{1,0},{2,1},{3,2},{4,3},{5,4},{6,5},{7,6},{8,7},{9,8},{10,9},{11,1... | collective-permute-start | bytes 319496 | tf_op jit(solution)/shard_map/ppermute | solution.py:17
  96.0 1.7 copy-start.1
  317.4 57.8 %copy-start.3 = (f32[128,1]{1,0:T(8,128)S(1)}, f32[128,1]{1,0:T(8,128)}, u32[]{:S(2)}) copy-start(f32[128,1]{1,0:T(8,128)} %constant.88.clone.3) | copy-start | bytes 1540
Sparse Core Ops, SparseCore 0:
  100.3 217.0 all-gather.2
